TPU v7x, 32 devices: a whole 2x2x4 slice. The times are simulated.
32 devices in a mesh: mp: 2 (over y), tx: 4 (over z), ty: 4 (over x, core).
Axes of the slice: x: 2, y: 2, z: 4, core: 2. Of those that a mesh axis runs over, the one named last changes fastest.
Arguments:
- models: float32 [2, 16, 64, 512], P('mp', None, 'ty', 'tx'), may hold values from -6 to 6
- direction: float32 [2, 16, 64, 512], P('mp', None, 'ty', 'tx'), may hold values from -6 to 6
- coupling: float32 [2], replicated, may hold values from 0.1 to 0.4
- tv_weight: float32 [2], replicated, may hold values from 0.5 to 2
Outputs:
- gradient: float32 [2, 16, 64, 512], P('mp', None, 'ty', 'tx')
- hessian_vector: float32 [2, 16, 64, 512], P('mp', None, 'ty', 'tx')
All inputs are finite; a program needn't handle non-finite values.
Results may differ from a plain program's by a relative error of at most 0.0001.
Values sent between devices are 32-bit elements; how exact they have to be, the bound alone decides.
No kernel may reach another device: no remote copies, remote signals or barrier semaphores. Data moves between devices by JAX's collectives and lax.ppermute only.
A program may use at most 64 MiB of HBM per device.

v0:
```python
import jax
import jax.numpy as jnp
from jax import lax
from jax.sharding import PartitionSpec as P

EPS_SQ = 0.25
SYM_PAIRS = ((0, 0), (1, 1), (2, 2), (0, 1), (0, 2), (1, 2))


def passed_along(array, axis, by):
    size = lax.axis_size(axis)
    pairs = [(i, i + by) for i in range(size) if 0 <= i + by < size]
    return lax.ppermute(array, axis, pairs)


def edge_masks(width_y, width_x):
    end_x = lax.axis_index("tx") == lax.axis_size("tx") - 1
    end_y = lax.axis_index("ty") == lax.axis_size("ty") - 1
    col_x = lax.broadcasted_iota(jnp.int32, (1, 1, width_x), 2)
    row_y = lax.broadcasted_iota(jnp.int32, (1, width_y, 1), 1)
    return ((col_x == width_x - 1) & end_x, (row_y == width_y - 1) & end_y)


def fields(tile, rim_x, rim_y):
    last_x, last_y = edge_masks(tile.shape[3], tile.shape[4])
    dx = jnp.concatenate([tile[..., 1:], rim_x], -1) - tile
    dx = jnp.where(last_x, 0.0, dx)
    dy = jnp.concatenate([tile[..., 1:, :], rim_y], -2) - tile
    dy = jnp.where(last_y, 0.0, dy)
    dz = jnp.concatenate(
        [tile[..., 1:, :, :] - tile[..., :-1, :, :], jnp.zeros_like(tile[..., :1, :, :])], -3
    )
    grads = jnp.stack([dx[:, 0], dy[:, 0], dz[:, 0]], 1)
    dirs = jnp.stack([dx[:, 1], dy[:, 1], dz[:, 1]], 1)
    return (grads, dirs)


def moments(grads, dirs, weights):
    wts = weights[:, None, None, None]
    rows = [jnp.sum(wts * grads[:, i] * grads[:, j], 0) for i, j in SYM_PAIRS]
    for i in range(3):
        for j in range(3):
            rows.append(jnp.sum(wts * dirs[:, i] * grads[:, j], 0))
    return jnp.stack(rows, 0)


def couple(moms, grad_own, dir_own):
    trace_m = moms[0] + moms[1] + moms[2]
    mat = [[moms[0], moms[3], moms[4]], [moms[3], moms[1], moms[5]], [moms[4], moms[5], moms[2]]]
    nat = [[moms[6 + 3 * i + j] for j in range(3)] for i in range(3)]
    trace_n = nat[0][0] + nat[1][1] + nat[2][2]
    g_parts = [grad_own[..., i, :, :, :] for i in range(3)]
    e_parts = [dir_own[..., i, :, :, :] for i in range(3)]
    cross_q = []
    cross_p = []
    for i in range(3):
        mg = mat[i][0] * g_parts[0] + mat[i][1] * g_parts[1] + mat[i][2] * g_parts[2]
        me = mat[i][0] * e_parts[0] + mat[i][1] * e_parts[1] + mat[i][2] * e_parts[2]
        ng = nat[i][0] * g_parts[0] + nat[i][1] * g_parts[1] + nat[i][2] * g_parts[2]
        cross_q.append(trace_m * g_parts[i] - mg)
        cross_p.append(trace_m * e_parts[i] - me + trace_n * g_parts[i] - ng)
    return (jnp.stack(cross_q, axis=-4), jnp.stack(cross_p, axis=-4))


def model_split(own, rim_x, rim_y, alpha, beta, own_weights):
    grads, dirs = fields(own, rim_x, rim_y)
    moms = lax.psum(moments(grads, dirs, own_weights), "mp")
    grad_own = grads[0]
    dir_own = dirs[0]
    cross_q, cross_p = couple(moms, grad_own, dir_own)
    size = jnp.sqrt(jnp.sum(grad_own * grad_own, 0) + EPS_SQ)[None]
    flux = jnp.stack(
        [beta * grad_own / size + alpha * cross_q, beta * dir_own / size + alpha * cross_p], 0
    )
    last_x, last_y = edge_masks(flux.shape[3], flux.shape[4])
    flux_x = jnp.where(last_x, 0.0, flux[:, 0])
    flux_y = jnp.where(last_y, 0.0, flux[:, 1])
    flux_z = flux[:, 2]
    flux_z = jnp.concatenate([flux_z[..., :-1, :, :], jnp.zeros_like(flux_z[..., :1, :, :])], -3)
    prev_x = passed_along(flux_x[..., -1:], "tx", 1)
    prev_y = passed_along(flux_y[..., -1:, :], "ty", 1)
    result = jnp.concatenate([prev_x, flux_x[..., :-1]], -1) - flux_x
    result = result + jnp.concatenate([prev_y, flux_y[..., :-1, :]], -2) - flux_y
    result = (
        result
        + jnp.concatenate([jnp.zeros_like(flux_z[..., :1, :, :]), flux_z[..., :-1, :, :]], -3)
        - flux_z
    )
    return (result[0][None], result[1][None])


def shards(models, direction, coupling, tv_weight):
    member = lax.axis_index("mp")
    own_weights = lax.dynamic_slice_in_dim(coupling, member, 1)
    alpha = own_weights[0]
    beta = lax.dynamic_slice_in_dim(tv_weight, member, 1)[0]
    own = jnp.stack([models, direction], 1)
    rim_x = passed_along(own[..., :1], "tx", -1)
    rim_y = passed_along(own[..., :1, :], "ty", -1)
    return model_split(own, rim_x, rim_y, alpha, beta, own_weights)


def solution(mesh):
    placed = (P("mp", None, "ty", "tx"), P("mp", None, "ty", "tx"), P(), P())
    return jax.shard_map(
        shards,
        mesh=mesh,
        in_specs=placed,
        out_specs=(P("mp", None, "ty", "tx"), P("mp", None, "ty", "tx")),
        check_vma=False,
    )
```

profile of v0, /device:TPU:0, one launch (start us, length us, event | category | flops | bytes accessed | tf_op | source)
XLA Modules:
  0.0 117.1 jit_solution(6490164148567552637)
XLA Ops:
  7.2 0.0 copy-start.1
  7.2 0.0 copy-start.2
  7.2 0.0 copy-start.5
  7.2 0.0 all-reduce.4.cloned.1.call-start
  7.2 0.9 fusion.75
  8.2 1.3 %collective-permute-start.1 = (f32[1,2,16,1,128]{4,3,2,1,0:T(1,128)S(1)}, f32[1,2,16,1,128]{4,3,2,1,0:T(1,128)S(1)}, u32[]{:S(2)}, u32[]{:S(2)}) collective-permute-start(f32[1,2,16,1,128]{4,3,2,1,0:T(1,128)S(1)} %fusion.75), channel_id=1, source_target_pairs={{1,0},{2,1},{3,2},{5,4},{6,5},{7,6},{9,8},{10,9},{11,10},{13,12},{... | collective-permute-start | bytes 49160 | tf_op jit(solution)/shard_map/ppermute | solution.py:13
  9.5 1.0 fusion.6
  10.5 1.3 %collective-permute-start = (f32[1,2,16,16,1]{4,3,2,1,0:T(8,128)S(1)}, f32[1,2,16,16,1]{4,3,2,1,0:T(8,128)S(1)}, u32[]{:S(2)}, u32[]{:S(2)}) collective-permute-start(f32[1,2,16,16,1]{4,3,2,1,0:T(8,128)S(1)} %fusion.6), channel_id=1, source_target_pairs={{4,0},{8,4},{12,8},{5,1},{9,5},{13,9},{6,2},{10,6},{14,10},{7,3},{... | collective-permute-start | bytes 6152 | tf_op jit(solution)/shard_map/ppermute | solution.py:13
  11.8 1.0 fusion.7
  12.8 1.1 fusion.5
  13.9 1.1 fusion.22
  15.0 0.0 copy-done.5
  15.1 0.6 dynamic_slice.7
  15.6 6.5 %collective-permute-done = f32[1,2,16,16,1]{4,3,2,1,0:T(8,128)S(1)} collective-permute-done((f32[1,2,16,16,1]{4,3,2,1,0:T(8,128)S(1)}, f32[1,2,16,16,1]{4,3,2,1,0:T(8,128)S(1)}, u32[]{:S(2)}, u32[]{:S(2)}) %collective-permute-start) | collective-permute-done | bytes 2080 | tf_op jit(solution)/shard_map/ppermute | solution.py:13
  22.2 0.0 collective-permute-done.1
  22.2 0.0 copy-done.1
  22.2 0.0 copy-done.2
  22.2 0.2 fusion.16
  22.3 0.7 fusion.24
  23.0 0.7 fusion.27
  23.7 0.7 fusion.29
  24.3 0.7 fusion.25
  25.0 0.7 fusion.26
  25.7 0.7 fusion.28
  26.3 0.7 fusion.72
  27.0 0.7 fusion.66
  27.7 0.7 fusion.54
  28.4 0.7 fusion.73
  29.0 0.7 fusion.67
  29.7 0.0 copy-start.6
  29.7 0.7 fusion.55
  30.4 0.7 fusion.74
  31.1 0.7 fusion.68
  31.7 0.7 fusion.56
  32.4 0.0 copy-start.3
  32.4 1.3 %copy-done.3 = f32[15,16,16,128]{3,2,1,0:T(8,128)} copy-done((f32[15,16,16,128]{3,2,1,0:T(8,128)}, f32[15,16,16,128]{3,2,1,0:T(8,128)S(1)}, u32[]{:S(2)}) %copy-start.3) | copy-done | bytes 1966104
  33.7 0.0 all-reduce.4.cloned.1.call-update
  33.7 0.0 copy-done.6
  33.7 0.6 dynamic_slice.6
  34.4 60.8 %all-reduce.4.cloned.1.call-done = f32[15,16,16,128]{3,2,1,0:T(8,128)} async-done(((f32[15,16,16,128]{3,2,1,0:T(8,128)}), f32[15,16,16,128]{3,2,1,0:T(8,128)}) %all-reduce.4.cloned.1.call-update) | async-done | bytes 1966096 | tf_op jit(solution)/shard_map/psum | solution.py:67
  95.2 0.0 copy-start
  95.2 1.6 %fusion.40 = (f32[1,1,16,16,128]{4,3,2,0,1:T(8,128)S(1)}, f32[1,16,16,128]{3,2,1,0:T(8,128)S(1)}, f32[1,16,16,128]{3,2,1,0:T(8,128)S(1)}) fusion(f32[15,16,16,128]{3,2,1,0:T(8,128)} %all-reduce.4.cloned.1.call-done, f32[1,2,16,16,128]{4,3,2,1,0:T(8,128)S(1)} %get-tuple-element.17, f32[1,2,16,16,128]{4,3,2,1,0:T(8,128)S(1)} %get-tuple-element.18, ...), kind=kLoop, calls=%fused_computation.79 | loop fusion | flops 622592 | bytes 2473984 | tf_op jit(solution)/shard_map/stack | solution.py:62
  96.8 0.4 copy-done
  97.2 0.1 fusion.36
  97.4 0.1 fusion.33
  97.5 0.1 fusion.59
  97.6 1.4 %fusion.1 = f32[1,3,16,16,128]{4,3,2,0,1:T(8,128)S(1)} fusion(f32[1,1,16,16,128]{4,3,2,1,0:T(8,128)S(1)} %get-tuple-element.6, f32[1,1,16,16,128]{4,3,2,1,0:T(8,128)S(1)} %get-tuple-element.8, f32[1,1,16,16,128]{4,3,2,1,0:T(8,128)S(1)} %fusion.59, f32[1,1,16,16,128]{4,3,2,1,0:T(8,128)S(1)} %get-tuple-element.20, ...), kind=kLoop, calls=%fused_computation.20 | loop fusion | flops 786432 | bytes 1310728 | tf_op jit(solution)/shard_map/add | solution.py:73
  99.0 1.4 %fusion.4 = f32[1,3,16,16,128]{4,3,2,0,1:T(8,128)S(1)} fusion(f32[1,1,16,16,128]{4,3,2,1,0:T(8,128)S(1)} %get-tuple-element.19, f32[1,1,16,16,128]{4,3,2,1,0:T(8,128)S(1)} %get-tuple-element.22, f32[1,1,16,16,128]{4,3,2,1,0:T(8,128)S(1)} %get-tuple-element.13, f32[1,1,16,16,128]{4,3,2,0,1:T(8,128)S(1)} %get-tuple-element.7, ...), kind=kLoop, calls=%fused_computation.24 | loop fusion | flops 786432 | bytes 1310728 | tf_op jit(solution)/shard_map/add | solution.py:73
  100.3 0.0 copy-start.4
  100.3 0.1 fusion.13
  100.4 0.1 slice.200
  100.6 3.4 %collective-permute-start.2 = (f32[2,16,16,1]{3,2,1,0:T(8,128)S(1)}, f32[2,16,16,1]{3,2,1,0:T(8,128)S(1)}, u32[]{:S(2)}, u32[]{:S(2)}) collective-permute-start(f32[2,16,16,1]{3,2,1,0:T(8,128)S(1)} %slice.200), channel_id=1, source_target_pairs={{0,4},{4,8},{8,12},{1,5},{5,9},{9,13},{2,6},{6,10},{10,14},{3,7},{... | collective-permute-start | bytes 6152 | tf_op jit(solution)/shard_map/ppermute | solution.py:13
  104.0 1.3 %collective-permute-start.3 = (f32[2,16,1,128]{3,2,1,0:T(1,128)S(1)}, f32[2,16,1,128]{3,2,1,0:T(1,128)S(1)}, u32[]{:S(2)}, u32[]{:S(2)}) collective-permute-start(f32[2,16,1,128]{3,2,1,0:T(1,128)S(1)} %slice.204), channel_id=1, source_target_pairs={{0,1},{1,2},{2,3},{4,5},{5,6},{6,7},{8,9},{9,10},{10,11},{12,13},{... | collective-permute-start | bytes 49160 | tf_op jit(solution)/shard_map/ppermute | solution.py:13
  105.4 4.0 %collective-permute-done.2 = f32[2,16,16,1]{3,2,1,0:T(8,128)S(1)} collective-permute-done((f32[2,16,16,1]{3,2,1,0:T(8,128)S(1)}, f32[2,16,16,1]{3,2,1,0:T(8,128)S(1)}, u32[]{:S(2)}, u32[]{:S(2)}) %collective-permute-start.2) | collective-permute-done | bytes 2080 | tf_op jit(solution)/shard_map/ppermute | solution.py:13
  109.3 0.0 collective-permute-done.3
  109.3 0.0 copy-done.4
  109.3 0.2 fusion.20
  109.5 0.7 fusion.76
  (9 shorter events, 0.2 us)
Async XLA Ops:
  7.2 15.0 %copy-start.1 = (f32[1,16,16,128]{3,2,1,0:T(8,128)S(1)}, f32[1,16,16,128]{3,2,1,0:T(8,128)}, u32[]{:S(2)}) copy-start(f32[1,16,16,128]{3,2,1,0:T(8,128)} %param.4) | copy-start | bytes 393220
  7.2 15.0 %copy-start.2 = (f32[1,16,16,128]{3,2,1,0:T(8,128)S(1)}, f32[1,16,16,128]{3,2,1,0:T(8,128)}, u32[]{:S(2)}) copy-start(f32[1,16,16,128]{3,2,1,0:T(8,128)} %param.5) | copy-start | bytes 393220
  7.2 7.9 %copy-start.5 = (f32[2]{0:T(128)S(1)}, f32[2]{0:T(128)}, u32[]{:S(2)}) copy-start(f32[2]{0:T(128)} %param.6) | copy-start | bytes 28
  7.2 88.0 %all-reduce.4.cloned.1.call-start = ((), (), s32[]{:S(2)}) async-start(), calls=%async_computation | async-start | bytes 3932160 | tf_op jit(solution)/shard_map/psum | solution.py:67
  8.2 14.0 %collective-permute-start.1 = (f32[1,2,16,1,128]{4,3,2,1,0:T(1,128)S(1)}, f32[1,2,16,1,128]{4,3,2,1,0:T(1,128)S(1)}, u32[]{:S(2)}, u32[]{:S(2)}) collective-permute-start(f32[1,2,16,1,128]{4,3,2,1,0:T(1,128)S(1)} %fusion.75), channel_id=1, source_target_pairs={{1,0},{2,1},{3,2},{5,4},{6,5},{7,6},{9,8},{10,9},{11,10},{13,12},{... | collective-permute-start | bytes 49160 | tf_op jit(solution)/shard_map/ppermute | solution.py:13
  10.5 11.7 %collective-permute-start = (f32[1,2,16,16,1]{4,3,2,1,0:T(8,128)S(1)}, f32[1,2,16,16,1]{4,3,2,1,0:T(8,128)S(1)}, u32[]{:S(2)}, u32[]{:S(2)}) collective-permute-start(f32[1,2,16,16,1]{4,3,2,1,0:T(8,128)S(1)} %fusion.6), channel_id=1, source_target_pairs={{4,0},{8,4},{12,8},{5,1},{9,5},{13,9},{6,2},{10,6},{14,10},{7,3},{... | collective-permute-start | bytes 6152 | tf_op jit(solution)/shard_map/ppermute | solution.py:13
  29.7 4.0 %copy-start.6 = (f32[2]{0:T(128)S(1)}, f32[2]{0:T(128)}, u32[]{:S(2)}) copy-start(f32[2]{0:T(128)} %param.7) | copy-start | bytes 28
  32.4 1.3 %copy-start.3 = (f32[15,16,16,128]{3,2,1,0:T(8,128)}, f32[15,16,16,128]{3,2,1,0:T(8,128)S(1)}, u32[]{:S(2)}) copy-start(f32[15,16,16,128]{3,2,1,0:T(8,128)S(1)} %fusion.56) | copy-start | bytes 5898244
  95.2 2.0 %copy-start = (f32[15,16,16,128]{3,2,1,0:T(8,128)S(1)}, f32[15,16,16,128]{3,2,1,0:T(8,128)}, u32[]{:S(2)}) copy-start(f32[15,16,16,128]{3,2,1,0:T(8,128)} %all-reduce.4.cloned.1.call-done) | copy-start | bytes 5898244
  100.3 9.0 %copy-start.4 = (pred[16]{0:T(512)(128)(4,1)S(1)}, pred[16]{0:T(512)(128)(4,1)}, u32[]{:S(2)}) copy-start(pred[16]{0:T(512)(128)(4,1)} %constant.30.clone.1) | copy-start | bytes 52
  100.6 8.8 %collective-permute-start.2 = (f32[2,16,16,1]{3,2,1,0:T(8,128)S(1)}, f32[2,16,16,1]{3,2,1,0:T(8,128)S(1)}, u32[]{:S(2)}, u32[]{:S(2)}) collective-permute-start(f32[2,16,16,1]{3,2,1,0:T(8,128)S(1)} %slice.200), channel_id=1, source_target_pairs={{0,4},{4,8},{8,12},{1,5},{5,9},{9,13},{2,6},{6,10},{10,14},{3,7},{... | collective-permute-start | bytes 6152 | tf_op jit(solution)/shard_map/ppermute | solution.py:13
  104.0 5.3 %collective-permute-start.3 = (f32[2,16,1,128]{3,2,1,0:T(1,128)S(1)}, f32[2,16,1,128]{3,2,1,0:T(1,128)S(1)}, u32[]{:S(2)}, u32[]{:S(2)}) collective-permute-start(f32[2,16,1,128]{3,2,1,0:T(1,128)S(1)} %slice.204), channel_id=1, source_target_pairs={{0,1},{1,2},{2,3},{4,5},{5,6},{6,7},{8,9},{9,10},{10,11},{12,13},{... | collective-permute-start | bytes 49160 | tf_op jit(solution)/shard_map/ppermute | solution.py:13
Sparse Core Ops, SparseCore 0:
  33.8 61.3 all-reduce.3
where the time goes:
time: 118 us; the launch traced here: 117 us
  waiting for transfers between devices  71.3 us (60%)
  other arithmetic  20.3 us (17%)
  between operations  14.4 us (12%)
  starting transfers between devices  7.32 us (6%)
  local copies, waits for them, and re-layouts  3.79 us (3%)
    psum x1, waiting for transfers between devices, model_split(): moms = lax.psum(moments(grads, dirs, own_weights), 'mp')  60.8 us
    ppermute x4, waiting for transfers between devices, passed_along(): return lax.ppermute(array, axis, pairs)  10.5 us
    unnamed x14, other arithmetic  9.27 us
    ppermute x4, starting transfers between devices, passed_along(): return lax.ppermute(array, axis, pairs)  7.28 us
    another operation x4, other arithmetic, shards(): own = jnp.stack([models, direction], 1)  4.02 us
  transfers between devices with their start and end apart: 5, of which 3 were waited for; matrix products, arithmetic and copies ran while one was open for 5% of the time, Pallas kernels for 0%

commit v1 on v0

--- a/solution.py
+++ b/solution.py
@@ -64,7 +64,7 @@
 
 def model_split(own, rim_x, rim_y, alpha, beta, own_weights):
     grads, dirs = fields(own, rim_x, rim_y)
-    moms = lax.psum(moments(grads, dirs, own_weights), "mp")
+    moms = jnp.sum(lax.all_gather(moments(grads, dirs, own_weights), "mp"), axis=0)
     grad_own = grads[0]
     dir_own = dirs[0]
     cross_q, cross_p = couple(moms, grad_own, dir_own)

time: 118 us -> 108 us (0.915)
  waiting for transfers between devices: 71.3 us -> 61.1 us
    psum x1 -> x0, waiting for transfers between devices: 60.8 us -> none  [model_split(): moms = lax.psum(moments(grads, dirs, own_weights), 'mp')]
    all_gather x0 -> x1, waiting for transfers between devices: none -> 53.2 us  [model_split(): lax.all_gather(moments(grads, dirs, own_weights), 'mp')]
    reduce_sum x0 -> x1, other arithmetic: none -> 2.62 us  [model_split(): jnp.sum(lax.all_gather(moments(grads, dirs, own_weights), 'mp'), axis=0)]
    ppermute x4, waiting for transfers between devices: 10.5 us -> 7.9 us  [passed_along(): return lax.ppermute(array, axis, pairs)]
    another operation x4, other arithmetic: 1.97 us -> 0.48 us  [couple(): return (jnp.stack(cross_q, axis=-4), jnp.stack(cross_p, axis=-4))]
    add x1 -> x0, other arithmetic: 1.36 us -> none  [model_split(): beta * grad_own / size + alpha * cross_q]
  transfers between devices with their start and end apart: 5 -> 5, of which waited for: 3 -> 3; matrix products, arithmetic and copies ran while one was open for 5% -> 6% of each run, Pallas kernels for 0% -> 0%
where the time goes in v1:
time: 108 us
  waiting for transfers between devices  61.1 us (57%)
  other arithmetic  20 us (19%)
  between operations  14.4 us (13%)
  starting transfers between devices  7.32 us (7%)
  local copies, waits for them, and re-layouts  4.66 us (4%)
    all_gather x1, waiting for transfers between devices, model_split(): lax.all_gather(moments(grads, dirs, own_weights), 'mp')  53.2 us
    unnamed x14, other arithmetic  9.27 us
    ppermute x4, waiting for transfers between devices, passed_along(): return lax.ppermute(array, axis, pairs)  7.9 us
    ppermute x4, starting transfers between devices, passed_along(): return lax.ppermute(array, axis, pairs)  7.28 us
    another operation x4, other arithmetic, shards(): own = jnp.stack([models, direction], 1)  4.02 us
    reduce_sum x1, other arithmetic, model_split(): jnp.sum(lax.all_gather(moments(grads, dirs, own_weights), 'mp'), axis=0)  2.62 us
  transfers between devices with their start and end apart: 5, of which 3 were waited for; matrix products, arithmetic and copies ran while one was open for 6% of the time, Pallas kernels for 0%

profile of v1, /device:TPU:0, one launch (start us, length us, event | category | flops | bytes accessed | tf_op | source)
XLA Modules:
  0.0 107.5 jit_solution(2361231587088614025)
XLA Ops:
  7.2 0.0 copy-start
  7.2 0.0 copy-start.1
  7.2 0.0 copy-start.5
  7.2 0.0 all-gather.3.cloned.1.call-start
  7.2 1.0 fusion.4
  8.3 1.3 %collective-permute-start = (f32[1,2,16,16,1]{4,3,2,1,0:T(8,128)S(1)}, f32[1,2,16,16,1]{4,3,2,1,0:T(8,128)S(1)}, u32[]{:S(2)}, u32[]{:S(2)}) collective-permute-start(f32[1,2,16,16,1]{4,3,2,1,0:T(8,128)S(1)} %fusion.4), channel_id=1, source_target_pairs={{4,0},{8,4},{12,8},{5,1},{9,5},{13,9},{6,2},{10,6},{14,10},{7,3},{... | collective-permute-start | bytes 6152 | tf_op jit(solution)/shard_map/ppermute | solution.py:13
  9.6 0.9 fusion.73
  10.5 1.3 %collective-permute-start.1 = (f32[1,2,16,1,128]{4,3,2,1,0:T(1,128)S(1)}, f32[1,2,16,1,128]{4,3,2,1,0:T(1,128)S(1)}, u32[]{:S(2)}, u32[]{:S(2)}) collective-permute-start(f32[1,2,16,1,128]{4,3,2,1,0:T(1,128)S(1)} %fusion.73), channel_id=1, source_target_pairs={{1,0},{2,1},{3,2},{5,4},{6,5},{7,6},{9,8},{10,9},{11,10},{13,12},{... | collective-permute-start | bytes 49160 | tf_op jit(solution)/shard_map/ppermute | solution.py:13
  11.8 1.1 %fusion.3 = f32[1,2,16,16,127]{4,3,2,1,0:T(8,128)S(1)} fusion(f32[1,1,16,16,128]{4,3,2,1,0:T(8,128)} %bitcast.236, f32[1,1,16,16,128]{4,3,2,1,0:T(8,128)} %bitcast.242), kind=kLoop, calls=%fused_computation.25 | loop fusion | flops 65024 | bytes 522240 | tf_op jit(solution)/shard_map/stack | solution.py:97
  12.9 1.0 fusion.5
  13.9 1.1 %fusion.20 = f32[1,2,15,16,128]{4,3,2,1,0:T(8,128)S(1)} fusion(f32[1,1,16,16,128]{4,3,2,1,0:T(8,128)} %bitcast.238, f32[1,1,16,16,128]{4,3,2,1,0:T(8,128)} %bitcast.244), kind=kLoop, calls=%fused_computation.48 | loop fusion | flops 184320 | bytes 507904 | tf_op jit(solution)/shard_map/sub | solution.py:31
  15.0 0.0 copy-done.5
  15.1 0.6 dynamic_slice.7
  15.6 3.9 %collective-permute-done = f32[1,2,16,16,1]{4,3,2,1,0:T(8,128)S(1)} collective-permute-done((f32[1,2,16,16,1]{4,3,2,1,0:T(8,128)S(1)}, f32[1,2,16,16,1]{4,3,2,1,0:T(8,128)S(1)}, u32[]{:S(2)}, u32[]{:S(2)}) %collective-permute-start) | collective-permute-done | bytes 2080 | tf_op jit(solution)/shard_map/ppermute | solution.py:13
  19.6 0.0 collective-permute-done.1
  19.6 0.0 copy-done
  19.6 0.0 copy-done.1
  19.6 0.2 fusion.14
  19.7 0.7 fusion.22
  20.4 0.7 fusion.25
  21.1 0.7 fusion.27
  21.7 0.7 fusion.23
  22.4 0.7 fusion.24
  23.1 0.7 fusion.26
  23.7 0.7 fusion.70
  24.4 0.7 fusion.64
  25.1 0.7 fusion.52
  25.8 0.7 fusion.71
  26.4 0.7 fusion.65
  27.1 0.0 copy-start.6
  27.1 0.7 fusion.53
  27.8 0.7 fusion.72
  28.4 0.7 fusion.66
  29.1 0.7 fusion.54
  29.8 0.0 copy-start.2
  29.8 1.3 %copy-done.2 = f32[15,16,16,128]{3,2,1,0:T(8,128)} copy-done((f32[15,16,16,128]{3,2,1,0:T(8,128)}, f32[15,16,16,128]{3,2,1,0:T(8,128)S(1)}, u32[]{:S(2)}) %copy-start.2) | copy-done | bytes 1966104
  31.1 0.0 all-gather.3.cloned.1.call-update
  31.1 0.0 copy-done.6
  31.1 0.6 dynamic_slice.6
  31.7 0.7 fusion.75
  32.5 53.2 %all-gather.3.cloned.1.call-done = f32[30,16,16,128]{3,2,1,0:T(8,128)} async-done(((f32[15,16,16,128]{3,2,1,0:T(8,128)}), f32[30,16,16,128]{3,2,1,0:T(8,128)}) %all-gather.3.cloned.1.call-update) | async-done | bytes 3932176 | tf_op jit(solution)/shard_map/all_gather | solution.py:67
  85.7 2.6 %reduce_sum.20 = f32[15,16,16,128]{3,2,1,0:T(8,128)S(1)} reduce(f32[2,15,16,16,128]{4,3,2,1,0:T(8,128)} %bitcast.247, f32[]{:T(128)} %constant.9.clone.1), dimensions={0}, to_apply=%region_1.2 | reduce | flops 491520 | bytes 5898244 | tf_op jit(solution)/shard_map/reduce_sum | solution.py:67
  88.3 0.1 fusion.38
  88.5 0.1 fusion.57
  88.5 0.0 copy-start.3
  88.6 0.1 fusion.34
  88.7 0.1 fusion.31
  88.9 0.6 copy-done.3
  89.5 1.3 %fusion.2 = (f32[1,3,16,16,128]{4,3,2,1,0:T(8,128)S(1)}, f32[1,3,16,16,128]{4,3,2,1,0:T(8,128)S(1)}) fusion(f32[1,1,16,16,128]{4,3,2,1,0:T(8,128)S(1)} %get-tuple-element.19, f32[1,1,16,16,128]{4,3,2,1,0:T(8,128)S(1)} %copy-done.3, f32[1,1,16,16,128]{4,3,2,1,0:T(8,128)S(1)} %get-tuple-element.13, f32[1,1,16,16,128]{4,3,2,1,0:T(8,128)S(1)} %get-tuple-element.7, ...), kind=kLoop, calls=%fused_computation.22 | loop fusion | flops 1572864 | bytes 2490376 | tf_op jit(solution)/shard_map/add | solution.py:73
  90.8 0.0 copy-start.4
  90.8 0.1 fusion.11
  90.9 0.1 slice.200
  91.0 3.4 %collective-permute-start.2 = (f32[2,16,16,1]{3,2,1,0:T(8,128)S(1)}, f32[2,16,16,1]{3,2,1,0:T(8,128)S(1)}, u32[]{:S(2)}, u32[]{:S(2)}) collective-permute-start(f32[2,16,16,1]{3,2,1,0:T(8,128)S(1)} %slice.200), channel_id=1, source_target_pairs={{0,4},{4,8},{8,12},{1,5},{5,9},{9,13},{2,6},{6,10},{10,14},{3,7},{... | collective-permute-start | bytes 6152 | tf_op jit(solution)/shard_map/ppermute | solution.py:13
  94.5 1.3 %collective-permute-start.3 = (f32[2,16,1,128]{3,2,1,0:T(1,128)S(1)}, f32[2,16,1,128]{3,2,1,0:T(1,128)S(1)}, u32[]{:S(2)}, u32[]{:S(2)}) collective-permute-start(f32[2,16,1,128]{3,2,1,0:T(1,128)S(1)} %slice.204), channel_id=1, source_target_pairs={{0,1},{1,2},{2,3},{4,5},{5,6},{6,7},{8,9},{9,10},{10,11},{12,13},{... | collective-permute-start | bytes 49160 | tf_op jit(solution)/shard_map/ppermute | solution.py:13
  95.8 4.0 %collective-permute-done.2 = f32[2,16,16,1]{3,2,1,0:T(8,128)S(1)} collective-permute-done((f32[2,16,16,1]{3,2,1,0:T(8,128)S(1)}, f32[2,16,16,1]{3,2,1,0:T(8,128)S(1)}, u32[]{:S(2)}, u32[]{:S(2)}) %collective-permute-start.2) | collective-permute-done | bytes 2080 | tf_op jit(solution)/shard_map/ppermute | solution.py:13
  99.8 0.0 collective-permute-done.3
  99.8 0.0 copy-done.4
  99.8 0.2 fusion.18
  100.0 0.7 fusion.74
  (8 shorter events, 0.2 us)
Async XLA Ops:
  7.2 12.4 %copy-start = (f32[1,16,16,128]{3,2,1,0:T(8,128)S(1)}, f32[1,16,16,128]{3,2,1,0:T(8,128)}, u32[]{:S(2)}) copy-start(f32[1,16,16,128]{3,2,1,0:T(8,128)} %param.4) | copy-start | bytes 393220
  7.2 12.4 %copy-start.1 = (f32[1,16,16,128]{3,2,1,0:T(8,128)S(1)}, f32[1,16,16,128]{3,2,1,0:T(8,128)}, u32[]{:S(2)}) copy-start(f32[1,16,16,128]{3,2,1,0:T(8,128)} %param.5) | copy-start | bytes 393220
  7.2 7.9 %copy-start.5 = (f32[2]{0:T(128)S(1)}, f32[2]{0:T(128)}, u32[]{:S(2)}) copy-start(f32[2]{0:T(128)} %param.6) | copy-start | bytes 28
  7.2 78.5 %all-gather.3.cloned.1.call-start = ((), (), s32[]{:S(2)}) async-start(), calls=%async_computation | async-start | bytes 5898240 | tf_op jit(solution)/shard_map/all_gather | solution.py:67
  8.3 11.3 %collective-permute-start = (f32[1,2,16,16,1]{4,3,2,1,0:T(8,128)S(1)}, f32[1,2,16,16,1]{4,3,2,1,0:T(8,128)S(1)}, u32[]{:S(2)}, u32[]{:S(2)}) collective-permute-start(f32[1,2,16,16,1]{4,3,2,1,0:T(8,128)S(1)} %fusion.4), channel_id=1, source_target_pairs={{4,0},{8,4},{12,8},{5,1},{9,5},{13,9},{6,2},{10,6},{14,10},{7,3},{... | collective-permute-start | bytes 6152 | tf_op jit(solution)/shard_map/ppermute | solution.py:13
  10.5 9.1 %collective-permute-start.1 = (f32[1,2,16,1,128]{4,3,2,1,0:T(1,128)S(1)}, f32[1,2,16,1,128]{4,3,2,1,0:T(1,128)S(1)}, u32[]{:S(2)}, u32[]{:S(2)}) collective-permute-start(f32[1,2,16,1,128]{4,3,2,1,0:T(1,128)S(1)} %fusion.73), channel_id=1, source_target_pairs={{1,0},{2,1},{3,2},{5,4},{6,5},{7,6},{9,8},{10,9},{11,10},{13,12},{... | collective-permute-start | bytes 49160 | tf_op jit(solution)/shard_map/ppermute | solution.py:13
  27.1 4.0 %copy-start.6 = (f32[2]{0:T(128)S(1)}, f32[2]{0:T(128)}, u32[]{:S(2)}) copy-start(f32[2]{0:T(128)} %param.7) | copy-start | bytes 28
  29.8 1.3 %copy-start.2 = (f32[15,16,16,128]{3,2,1,0:T(8,128)}, f32[15,16,16,128]{3,2,1,0:T(8,128)S(1)}, u32[]{:S(2)}) copy-start(f32[15,16,16,128]{3,2,1,0:T(8,128)S(1)} %fusion.54) | copy-start | bytes 5898244
  88.5 0.9 copy-start.3
  90.8 9.0 %copy-start.4 = (pred[16]{0:T(512)(128)(4,1)S(1)}, pred[16]{0:T(512)(128)(4,1)}, u32[]{:S(2)}) copy-start(pred[16]{0:T(512)(128)(4,1)} %constant.30.clone.1) | copy-start | bytes 52
  91.0 8.8 %collective-permute-start.2 = (f32[2,16,16,1]{3,2,1,0:T(8,128)S(1)}, f32[2,16,16,1]{3,2,1,0:T(8,128)S(1)}, u32[]{:S(2)}, u32[]{:S(2)}) collective-permute-start(f32[2,16,16,1]{3,2,1,0:T(8,128)S(1)} %slice.200), channel_id=1, source_target_pairs={{0,4},{4,8},{8,12},{1,5},{5,9},{9,13},{2,6},{6,10},{10,14},{3,7},{... | collective-permute-start | bytes 6152 | tf_op jit(solution)/shard_map/ppermute | solution.py:13
  94.5 5.3 %collective-permute-start.3 = (f32[2,16,1,128]{3,2,1,0:T(1,128)S(1)}, f32[2,16,1,128]{3,2,1,0:T(1,128)S(1)}, u32[]{:S(2)}, u32[]{:S(2)}) collective-permute-start(f32[2,16,1,128]{3,2,1,0:T(1,128)S(1)} %slice.204), channel_id=1, source_target_pairs={{0,1},{1,2},{2,3},{4,5},{5,6},{6,7},{8,9},{9,10},{10,11},{12,13},{... | collective-permute-start | bytes 49160 | tf_op jit(solution)/shard_map/ppermute | solution.py:13
Sparse Core Ops, SparseCore 0:
  31.2 54.4 all-gather.2
